TPU v7x, 512 devices: a whole 4x8x8 slice. The times are simulated.
512 devices in a mesh: blk: 64 (over x, z, y_hi), dp: 8 (over y_lo, core).
Axes of the slice: x: 4, y: 8 (y_hi: 2, y_lo: 4; y = y_hi * 4 + y_lo), z: 8, core: 2. Of those that a mesh axis runs over, the one named last changes fastest.
Arguments:
- input_field: bfloat16 [262144, 2048], P('blk', 'dp'), may hold values from -6 to 6
- target_field: bfloat16 [262144, 2048], P('blk', 'dp'), may hold values from -6 to 6
- first_factor: bfloat16 [256, 1024, 256], P('dp', 'blk'), may hold values from -0.375 to 0.375
- second_factor: bfloat16 [256, 1024, 256], P('dp', 'blk'), may hold values from -0.375 to 0.375
Outputs:
- first_grad: bfloat16 [256, 1024, 256], P('dp', 'blk')
- second_grad: bfloat16 [256, 1024, 256], P('dp', 'blk')
All inputs are finite; a program needn't handle non-finite values.
Results may differ from a plain program's by a relative error of at most 0.012.
Values may be sent and summed in bfloat16 or wider, within the bound.
No kernel may reach another device: no remote copies, remote signals or barrier semaphores. Data moves between devices by JAX's collectives and lax.ppermute only.
A program may use at most 64 MiB of HBM per device.

v0:
```python
import math
import jax
import jax.numpy as jnp
from jax import lax
from jax.sharding import PartitionSpec as P

NB = 1024
BS = 256
tanh_scale = 0.7978845608028654
cubic_coef = 0.044715


def gelu_value(values):
    inner = jnp.tanh(tanh_scale * (values + cubic_coef * values * values * values))
    return 0.5 * values * (1.0 + inner)


def gelu_slope(values):
    inner = jnp.tanh(tanh_scale * (values + cubic_coef * values * values * values))
    return 0.5 * (1.0 + inner) + 0.5 * values * (1.0 - inner * inner) * tanh_scale * (
        1.0 + 3.0 * cubic_coef * values * values
    )


def shards(input_field, target_field, first_factor, second_factor):
    block_count = first_factor.shape[1]
    block_size = first_factor.shape[2]
    second_rows_local = second_factor.shape[0]
    row_count = input_field.shape[1]
    replica_count = lax.axis_size("dp")
    group_count = NB // BS
    inner_count = block_count // group_count
    scale_factor = 1.0 / math.sqrt(row_count * replica_count)
    inputs = input_field.reshape(block_count, block_size, row_count)
    first_full = lax.all_gather(first_factor, "dp", axis=0, tiled=True)
    pre_act = jnp.einsum("bkr,kbi->bir", inputs, first_full, preferred_element_type=jnp.float32)
    activated = gelu_value(pre_act).astype(jnp.bfloat16)
    received = lax.all_to_all(activated, "blk", split_axis=1, concat_axis=0, tiled=True)
    permuted = received.reshape(group_count, block_size, inner_count, row_count)
    targets = target_field.reshape(inner_count, group_count, block_size, row_count)
    piece_rows = lax.all_gather(second_factor, "dp", axis=0, tiled=True)
    count = piece_rows.shape[0]
    permuted_part = permuted
    split_part = piece_rows.reshape(count, inner_count, group_count, block_size)
    predicted = jnp.einsum(
        "gcir,cigj->igjr", permuted_part, split_part, preferred_element_type=jnp.float32
    )
    residual = ((predicted - targets.astype(jnp.float32)) * scale_factor).astype(jnp.bfloat16)
    piece_rows = lax.all_gather(second_factor, "dp", axis=0, tiled=True)
    count = piece_rows.shape[0]
    split_part = piece_rows.reshape(count, inner_count, group_count, block_size)
    permuted_grad = jnp.einsum(
        "cigj,igjr->gcir", split_part, residual, preferred_element_type=jnp.float32
    ).astype(jnp.bfloat16)
    permuted_part = permuted
    term = jnp.einsum(
        "gcir,igjr->cigj", permuted_part, residual, preferred_element_type=jnp.float32
    )
    second_out = lax.psum_scatter(
        term.reshape(second_rows_local * lax.axis_size("dp"), block_count, block_size).astype(
            jnp.bfloat16
        ),
        "dp",
        scatter_dimension=0,
        tiled=True,
    )
    sending = permuted_grad.reshape(group_count * block_size, inner_count, row_count)
    activated_grad = lax.all_to_all(sending, "blk", split_axis=0, concat_axis=1, tiled=True)
    pre_grad = (activated_grad.astype(jnp.float32) * gelu_slope(pre_act)).astype(jnp.bfloat16)
    first_sum = lax.psum_scatter(
        jnp.einsum("bkr,bir->kbi", inputs, pre_grad, preferred_element_type=jnp.float32).astype(
            jnp.bfloat16
        ),
        "dp",
        scatter_dimension=0,
        tiled=True,
    )
    return (first_sum, second_out)


def solution(mesh):
    return jax.shard_map(
        shards,
        mesh=mesh,
        in_specs=(P("blk", "dp"), P("blk", "dp"), P("dp", "blk", None), P("dp", "blk", None)),
        out_specs=(P("dp", "blk", None), P("dp", "blk", None)),
        check_vma=False,
    )
```

profile of v0, /device:TPU:2, one launch (start us, length us, event | category | flops | bytes accessed | tf_op | source)
XLA Modules:
  0.0 308.1 jit_solution(16598214252673159265)
XLA Ops:
  7.2 0.0 copy-start
  7.2 0.0 all-gather.3.cloned.1.call-start
  7.2 1.9 copy.40
  9.1 0.0 all-gather.3.cloned.1.call-update
  9.1 47.8 %all-gather.3.cloned.1.call-done = bf16[256,16,256]{2,0,1:T(8,128)(2,1)} async-done(((bf16[32,16,256]{2,0,1:T(8,128)(2,1)}), bf16[256,16,256]{2,0,1:T(8,128)(2,1)}) %all-gather.3.cloned.1.call-update) | async-done | bytes 2097168 | tf_op jit(solution)/shard_map/all_gather | solution.py:35
  56.9 0.0 copy-done
  56.9 5.2 %multiply_convert_fusion = (bf16[16,256,256]{2,1,0:T(8,128)(2,1)S(1)}, f32[16,256,256]{2,1,0:T(8,128)}) fusion(bf16[256,16,256]{2,0,1:T(8,128)(2,1)} %all-gather.3.cloned.1.call-done, bf16[16,256,256]{2,1,0:T(8,128)(2,1)S(1)} %bitcast.33), kind=kOutput, calls=%fused_computation.13 | convolution fusion | flops 546308096 | bytes 10485760 | tf_op jit(solution)/shard_map/bkr,kbi->bir/dot_general | solution.py:36
  62.2 2.5 copy.41
  64.7 14.5 %all-to-all-start = ((bf16[16,256,256]{2,0,1:T(8,128)(2,1)}), bf16[16,256,256]{2,0,1:T(8,128)(2,1)}, u32[]{:S(2)}, u32[]{:S(2)}) async-start(bf16[16,256,256]{2,0,1:T(8,128)(2,1)} %copy.41), calls=%async_computation | async-start | bytes 4194304 | tf_op jit(solution)/shard_map/all_to_all | solution.py:38
  79.2 0.0 all-gather.5.cloned.1.call-start
  79.3 0.7 all-gather.5.cloned.1.call-update
  80.0 4.6 %copy.45 = f32[4,4,256,256]{2,3,1,0:T(8,128)} copy(bf16[4,4,256,256]{3,2,1,0:T(8,128)(2,1)} %bitcast.42) | data formatting | bytes 6291456 | tf_op jit(solution)/shard_map/convert_element_type | solution.py:48
  84.5 61.2 %all-gather.5.cloned.1.call-done = bf16[256,16,256]{2,1,0:T(8,128)(2,1)} async-done(((bf16[32,16,256]{2,1,0:T(8,128)(2,1)}), bf16[256,16,256]{2,1,0:T(8,128)(2,1)}) %all-gather.5.cloned.1.call-update) | async-done | bytes 2097168 | tf_op jit(solution)/shard_map/all_gather | solution.py:41
  145.8 3.6 %copy.43 = bf16[256,16,256]{2,0,1:T(8,128)(2,1)} copy(bf16[256,16,256]{2,1,0:T(8,128)(2,1)} %all-gather.5.cloned.1.call-done) | data formatting | bytes 4194304 | tf_op jit(solution)/shard_map/all_gather | solution.py:41
  149.4 0.0 all-to-all-done
  149.4 0.0 copy-start.2
  149.4 1.9 copy.42
  151.3 0.0 copy-start.1
  151.3 0.9 copy-done.2
  152.2 0.0 copy-start.4
  152.2 2.8 fusion.8
  155.0 0.0 copy-done.1
  155.0 0.0 copy-done.4
  155.0 0.0 copy-start.3
  155.0 0.7 convert_bitcast_fusion.2
  155.8 0.1 copy.48
  155.9 0.4 copy-done.3
  156.4 3.0 copy.49
  159.3 12.1 %all-to-all-start.1 = ((bf16[1024,4,256]{2,1,0:T(4,128)(2,1)}), bf16[1024,4,256]{2,1,0:T(4,128)(2,1)}, u32[]{:S(2)}, u32[]{:S(2)}) async-start(bf16[1024,4,256]{2,1,0:T(4,128)(2,1)} %copy.49), calls=%async_computation.1 | async-start | bytes 4194304 | tf_op jit(solution)/shard_map/all_to_all | solution.py:68
  171.4 0.0 reduce-scatter.5.cloned.1.call-start
  171.5 4.3 %convolution_convert_fusion = bf16[4,4,256,256]{3,2,1,0:T(8,128)(2,1)} fusion(bf16[4,4,256,256]{2,3,1,0:T(8,128)(2,1)} %copy-done.3, bf16[4,256,4,256]{3,1,0,2:T(8,128)(2,1)} %bitcast.36), kind=kOutput, calls=%fused_computation.20 | convolution fusion | flops 537919488 | bytes 6291456 | tf_op jit(solution)/shard_map/gcir,igjr->cigj/dot_general | solution.py:56
  175.8 4.5 %copy.54 = bf16[256,16,256]{2,1,0:T(8,128)(2,1)} copy(bf16[256,16,256]{0,2,1:T(8,128)(2,1)} %bitcast.39) | data formatting | bytes 4194304 | tf_op jit(solution)/shard_map/convert_element_type | solution.py:60
  180.3 0.0 reduce-scatter.5.cloned.1.call-update
  180.3 0.2 reduce-scatter.3.cloned.1.call-start
  180.6 45.9 %all-to-all-done.1 = bf16[1024,4,256]{2,1,0:T(4,128)(2,1)} async-done(((bf16[1024,4,256]{2,1,0:T(4,128)(2,1)}), bf16[1024,4,256]{2,1,0:T(4,128)(2,1)}, u32[]{:S(2)}, u32[]{:S(2)}) %all-to-all-start.1) | async-done | bytes 2097184 | tf_op jit(solution)/shard_map/all_to_all | solution.py:68
  226.4 1.9 copy.50
  228.3 0.6 convert_bitcast_fusion
  228.9 4.7 %copy.51 = f32[16,64,4,256]{3,2,1,0:T(4,128)} copy(f32[16,64,4,256]{3,0,1,2:T(8,128)S(1)} %convert_bitcast_fusion) | data formatting | bytes 8388608 | tf_op jit(solution)/shard_map/convert_element_type | solution.py:69
  233.6 5.4 %reshape.32 = f32[16,256,256]{2,1,0:T(8,128)} reshape(f32[16,64,4,256]{3,2,1,0:T(4,128)} %copy.51) | data formatting | bytes 8388608 | tf_op jit(solution)/shard_map/convert_element_type | solution.py:69
  238.9 7.7 %convert_bitcast_fusion.1 = bf16[256,16,256]{0,2,1:T(8,128)(2,1)} fusion(bf16[16,256,256]{2,1,0:T(8,128)(2,1)S(1)} %bitcast.34, f32[16,256,256]{2,1,0:T(8,128)} %reshape.32, f32[16,256,256]{2,1,0:T(8,128)} %get-tuple-element.7), kind=kOutput, calls=%fused_computation.17 | convolution fusion | flops 557842432 | bytes 12582912 | tf_op jit(solution)/shard_map/bkr,bir->kbi/dot_general | solution.py:71
  246.7 4.6 %copy.52 = bf16[256,16,256]{2,1,0:T(8,128)(2,1)} copy(bf16[256,16,256]{0,2,1:T(8,128)(2,1)} %convert_bitcast_fusion.1) | data formatting | bytes 4194304 | tf_op jit(solution)/shard_map/convert_element_type | solution.py:71
  251.3 0.0 reduce-scatter.3.cloned.1.call-update
  251.3 0.0 reduce-scatter.5.cloned.1.call-done
  251.3 50.3 %reduce-scatter.3.cloned.1.call-done = bf16[32,16,256]{2,1,0:T(8,128)(2,1)} async-done(((bf16[256,16,256]{2,1,0:T(8,128)(2,1)}), bf16[32,16,256]{2,1,0:T(8,128)(2,1)}) %reduce-scatter.3.cloned.1.call-update) | async-done | bytes 262160 | tf_op jit(solution)/shard_map/reduce_scatter | solution.py:70
Async XLA Ops:
  7.2 49.8 %copy-start = (bf16[4096,256]{1,0:T(8,128)(2,1)S(1)}, bf16[4096,256]{1,0:T(8,128)(2,1)}, u32[]{:S(2)}) copy-start(bf16[4096,256]{1,0:T(8,128)(2,1)} %param.4) | copy-start | bytes 6291460
  7.2 49.8 %all-gather.3.cloned.1.call-start = ((), (), s32[]{:S(2)}) async-start(), calls=%async_computation.4 | async-start | bytes 2359296 | tf_op jit(solution)/shard_map/all_gather | solution.py:35
  64.7 84.7 %all-to-all-start = ((bf16[16,256,256]{2,0,1:T(8,128)(2,1)}), bf16[16,256,256]{2,0,1:T(8,128)(2,1)}, u32[]{:S(2)}, u32[]{:S(2)}) async-start(bf16[16,256,256]{2,0,1:T(8,128)(2,1)} %copy.41), calls=%async_computation | async-start | bytes 4194304 | tf_op jit(solution)/shard_map/all_to_all | solution.py:38
  79.2 66.5 %all-gather.5.cloned.1.call-start = ((), (), s32[]{:S(2)}) async-start(), calls=%async_computation.5 | async-start | bytes 2359296 | tf_op jit(solution)/shard_map/all_gather | solution.py:41
  149.4 2.8 copy-start.2
  151.3 3.7 %copy-start.1 = (bf16[64,16,4,256]{3,1,0,2:T(8,128)(2,1)}, bf16[64,16,4,256]{3,1,0,2:T(8,128)(2,1)S(1)}, u32[]{:S(2)}) copy-start(bf16[64,16,4,256]{3,1,0,2:T(8,128)(2,1)S(1)} %copy.42) | copy-start | bytes 6291460
  152.2 2.8 copy-start.4
  155.0 1.3 copy-start.3
  159.3 67.1 %all-to-all-start.1 = ((bf16[1024,4,256]{2,1,0:T(4,128)(2,1)}), bf16[1024,4,256]{2,1,0:T(4,128)(2,1)}, u32[]{:S(2)}, u32[]{:S(2)}) async-start(bf16[1024,4,256]{2,1,0:T(4,128)(2,1)} %copy.49), calls=%async_computation.1 | async-start | bytes 4194304 | tf_op jit(solution)/shard_map/all_to_all | solution.py:68
  171.4 79.9 %reduce-scatter.5.cloned.1.call-start = ((), (), s32[]{:S(2)}) async-start(), calls=%async_computation.7 | async-start | bytes 2359296 | tf_op jit(solution)/shard_map/reduce_scatter | solution.py:59
  180.3 121.2 %reduce-scatter.3.cloned.1.call-start = ((), (), s32[]{:S(2)}) async-start(), calls=%async_computation.6 | async-start | bytes 2359296 | tf_op jit(solution)/shard_map/reduce_scatter | solution.py:70
Sparse Core Ops, SparseCore 0:
  10.7 46.2 all-gather.2
  82.2 63.5 all-gather.4
  180.5 59.4 reduce-scatter.4
  251.4 50.1 reduce-scatter.2
where the time goes:
time: 309 us; the launch traced here: 308 us
  waiting for transfers between devices  206 us (67%)
  local copies, waits for them, and re-layouts  40 us (13%)
  starting transfers between devices  27 us (9%)
  matrix products  20.8 us (7%)
  between operations  13.9 us (4%)
    all_gather x1, waiting for transfers between devices, shards(): piece_rows = lax.all_gather(second_factor, 'dp', axis=0, tiled=True)  61.2 us
    reduce_scatter x1, waiting for transfers between devices, shards(): lax.psum_scatter(jnp.einsum('bkr,bir->kbi', inputs, pre_grad, preferred_e...  50.3 us
    all_gather x1, waiting for transfers between devices, shards(): first_full = lax.all_gather(first_factor, 'dp', axis=0, tiled=True)  47.8 us
    all_to_all x1, waiting for transfers between devices, shards(): lax.all_to_all(sending, 'blk', split_axis=0, concat_axis=1, tiled=True)  45.9 us
    all_to_all x1, starting transfers between devices, shards(): lax.all_to_all(activated, 'blk', split_axis=1, concat_axis=0, tiled=True)  14.5 us
    all_to_all x1, starting transfers between devices, shards(): lax.all_to_all(sending, 'blk', split_axis=0, concat_axis=1, tiled=True)  12.1 us
    convert_element_type x2, local copies, waits for them, and re-layouts, shards(): activated_grad.astype(jnp.float32) * gelu_slope(pre_act)  10 us
    dot_general x1, matrix products, shards(): jnp.einsum('bkr,bir->kbi', inputs, pre_grad, preferred_element_type=jnp.f...  7.74 us
  transfers between devices with their start and end apart: 6, of which 4 were waited for; matrix products, arithmetic and copies ran while one was open for 14% of the time, Pallas kernels for 0%

commit v1 on v0

--- a/solution.py
+++ b/solution.py
@@ -38,7 +38,9 @@
     received = lax.all_to_all(activated, "blk", split_axis=1, concat_axis=0, tiled=True)
     permuted = received.reshape(group_count, block_size, inner_count, row_count)
     targets = target_field.reshape(inner_count, group_count, block_size, row_count)
-    piece_rows = lax.all_gather(second_factor, "dp", axis=0, tiled=True)
+    piece_rows = jnp.concatenate(
+        lax.all_to_all(jnp.stack([second_factor] * lax.axis_size("dp")), "dp", 0, 0), axis=0
+    )
     count = piece_rows.shape[0]
     permuted_part = permuted
     split_part = piece_rows.reshape(count, inner_count, group_count, block_size)

time: 309 us -> 327 us (1.058)
  starting transfers between devices: 27 us -> 36 us
  waiting for transfers between devices: 206 us -> 210 us
  matrix products: 20.8 us -> 24.3 us
    all_gather x1, waiting for transfers between devices: 61.2 us -> 8.86 us  [shards(): piece_rows = lax.all_gather(second_factor, 'dp', axis=0, tiled=True)]
    all_to_all x1, waiting for transfers between devices: 0.01 us -> 42.6 us  [shards(): lax.all_to_all(activated, 'blk', split_axis=1, concat_axis=0, tiled=True)]
    all_gather x1, waiting for transfers between devices: 47.8 us -> 66.2 us  [shards(): first_full = lax.all_gather(first_factor, 'dp', axis=0, tiled=True)]
    all_to_all x1, waiting for transfers between devices: 45.9 us -> 40.6 us  [shards(): lax.all_to_all(sending, 'blk', split_axis=0, concat_axis=1, tiled=True)]
    all_to_all x0 -> x1, starting transfers between devices: none -> 4.88 us  [shards(): lax.all_to_all(jnp.stack([second_factor] * lax.axis_size('dp')), 'dp', 0, 0)]
    reduce_scatter x1, waiting for transfers between devices: 0.02 us -> 4.81 us  [shards(): lax.psum_scatter(term.reshape(second_rows_local * lax.axis_size('dp'), bl...]
    reduce_scatter x1, waiting for transfers between devices: 50.3 us -> 46 us  [shards(): lax.psum_scatter(jnp.einsum('bkr,bir->kbi', inputs, pre_grad, preferred_e...]
    all_gather x1 -> x0, local copies, waits for them, and re-layouts: 3.63 us -> none  [shards(): piece_rows = lax.all_gather(second_factor, 'dp', axis=0, tiled=True)]
  transfers between devices with their start and end apart: 6 -> 7, of which waited for: 4 -> 6; matrix products, arithmetic and copies ran while one was open for 14% -> 18% of each run, Pallas kernels for 0% -> 0%
where the time goes in v1:
time: 327 us
  waiting for transfers between devices  210 us (64%)
  local copies, waits for them, and re-layouts  42.1 us (13%)
  starting transfers between devices  36 us (11%)
  matrix products  24.3 us (7%)
  between operations  13.8 us (4%)
    all_gather x1, waiting for transfers between devices, shards(): first_full = lax.all_gather(first_factor, 'dp', axis=0, tiled=True)  66.2 us
    reduce_scatter x1, waiting for transfers between devices, shards(): lax.psum_scatter(jnp.einsum('bkr,bir->kbi', inputs, pre_grad, preferred_e...  46 us
    all_to_all x1, waiting for transfers between devices, shards(): lax.all_to_all(activated, 'blk', split_axis=1, concat_axis=0, tiled=True)  42.6 us
    all_to_all x1, waiting for transfers between devices, shards(): lax.all_to_all(sending, 'blk', split_axis=0, concat_axis=1, tiled=True)  40.6 us
    all_to_all x1, starting transfers between devices, shards(): lax.all_to_all(activated, 'blk', split_axis=1, concat_axis=0, tiled=True)  16.4 us
    all_to_all x1, starting transfers between devices, shards(): lax.all_to_all(sending, 'blk', split_axis=0, concat_axis=1, tiled=True)  14.4 us
    convert_element_type x2, local copies, waits for them, and re-layouts, shards(): activated_grad.astype(jnp.float32) * gelu_slope(pre_act)  10 us
    all_gather x1, waiting for transfers between devices, shards(): piece_rows = lax.all_gather(second_factor, 'dp', axis=0, tiled=True)  8.86 us
  transfers between devices with their start and end apart: 7, of which 6 were waited for; matrix products, arithmetic and copies ran while one was open for 18% of the time, Pallas kernels for 0%

profile of v1, /device:TPU:2, one launch (start us, length us, event | category | flops | bytes accessed | tf_op | source)
XLA Modules:
  0.0 326.6 jit_solution(11313349092127051935)
XLA Ops:
  7.2 0.0 copy-start
  7.2 0.0 all-gather.3.cloned.1.call-start
  7.2 1.9 copy.42
  9.1 0.0 all-gather.3.cloned.1.call-update
  9.1 1.0 copy.45
  10.2 0.0 copy-start.3
  10.2 1.6 stack.2
  11.8 0.0 copy-done.3
  11.8 4.9 %all-to-all-start.1 = ((bf16[8,32,16,256]{3,1,2,0:T(8,128)(2,1)}), bf16[8,32,16,256]{3,1,2,0:T(8,128)(2,1)}, u32[]{:S(2)}, u32[]{:S(2)}) async-start(bf16[8,32,16,256]{3,1,2,0:T(8,128)(2,1)} %stack.2), calls=%async_computation.1 | async-start | bytes 4194304 | tf_op jit(solution)/shard_map/all_to_all | solution.py:42
  16.7 66.2 %all-gather.3.cloned.1.call-done = bf16[256,16,256]{2,0,1:T(8,128)(2,1)} async-done(((bf16[32,16,256]{2,0,1:T(8,128)(2,1)}), bf16[256,16,256]{2,0,1:T(8,128)(2,1)}) %all-gather.3.cloned.1.call-update) | async-done | bytes 2097168 | tf_op jit(solution)/shard_map/all_gather | solution.py:35
  82.8 0.0 copy-done
  82.8 5.2 %multiply_convert_fusion = (bf16[16,256,256]{2,1,0:T(8,128)(2,1)S(1)}, f32[16,256,256]{2,1,0:T(8,128)}) fusion(bf16[256,16,256]{2,0,1:T(8,128)(2,1)} %all-gather.3.cloned.1.call-done, bf16[16,256,256]{2,1,0:T(8,128)(2,1)S(1)} %bitcast.34), kind=kOutput, calls=%fused_computation.13 | convolution fusion | flops 546308096 | bytes 10485760 | tf_op jit(solution)/shard_map/bkr,kbi->bir/dot_general | solution.py:36
  88.0 2.5 copy.43
  90.6 0.0 all-to-all-done.1
  90.6 16.4 %all-to-all-start = ((bf16[16,256,256]{2,0,1:T(8,128)(2,1)}), bf16[16,256,256]{2,0,1:T(8,128)(2,1)}, u32[]{:S(2)}, u32[]{:S(2)}) async-start(bf16[16,256,256]{2,0,1:T(8,128)(2,1)} %copy.43), calls=%async_computation | async-start | bytes 4194304 | tf_op jit(solution)/shard_map/all_to_all | solution.py:38
  107.0 0.0 all-gather.5.cloned.1.call-start
  107.0 0.7 all-gather.5.cloned.1.call-update
  107.7 4.6 %copy.48 = f32[4,4,256,256]{2,3,1,0:T(8,128)} copy(bf16[4,4,256,256]{3,2,1,0:T(8,128)(2,1)} %bitcast.42) | data formatting | bytes 6291456 | tf_op jit(solution)/shard_map/convert_element_type | solution.py:50
  112.3 3.1 copy.46
  115.4 42.6 %all-to-all-done = bf16[16,256,256]{2,0,1:T(8,128)(2,1)} async-done(((bf16[16,256,256]{2,0,1:T(8,128)(2,1)}), bf16[16,256,256]{2,0,1:T(8,128)(2,1)}, u32[]{:S(2)}, u32[]{:S(2)}) %all-to-all-start) | async-done | bytes 2097184 | tf_op jit(solution)/shard_map/all_to_all | solution.py:38
  158.0 0.0 copy-start.2
  158.0 1.9 copy.44
  159.9 0.0 copy-start.1
  159.9 1.3 copy-done.1
  161.3 0.0 copy-done.2
  161.3 4.0 %fusion.8 = bf16[4,4,256,256]{2,3,1,0:T(8,128)(2,1)} fusion(f32[4,4,256,256]{2,3,1,0:T(8,128)S(1)} %copy-done.2, bf16[4,256,4,256]{3,1,0,2:T(8,128)(2,1)S(1)} %bitcast.36, bf16[256,4,4,256]{3,0,2,1:T(8,128)(2,1)} %bitcast.38), kind=kOutput, calls=%fused_computation.12 | convolution fusion | flops 540016640 | bytes 10485760 | tf_op jit(solution)/shard_map/gcir,cigj->igjr/dot_general | solution.py:47
  165.2 8.9 %all-gather.5.cloned.1.call-done = bf16[256,16,256]{2,0,1:T(8,128)(2,1)} async-done(((bf16[32,16,256]{2,0,1:T(8,128)(2,1)}), bf16[256,16,256]{2,0,1:T(8,128)(2,1)}) %all-gather.5.cloned.1.call-update) | async-done | bytes 2097168 | tf_op jit(solution)/shard_map/all_gather | solution.py:51
  174.1 3.0 convert_bitcast_fusion.2
  177.1 0.1 copy.52
  177.2 3.0 copy.53
  180.2 14.4 %all-to-all-start.2 = ((bf16[1024,4,256]{2,1,0:T(4,128)(2,1)}), bf16[1024,4,256]{2,1,0:T(4,128)(2,1)}, u32[]{:S(2)}, u32[]{:S(2)}) async-start(bf16[1024,4,256]{2,1,0:T(4,128)(2,1)} %copy.53), calls=%async_computation.2 | async-start | bytes 4194304 | tf_op jit(solution)/shard_map/all_to_all | solution.py:70
  194.6 0.0 reduce-scatter.5.cloned.1.call-start
  194.6 4.3 %convolution_convert_fusion = bf16[4,4,256,256]{3,2,1,0:T(8,128)(2,1)} fusion(bf16[4,4,256,256]{2,3,1,0:T(8,128)(2,1)} %fusion.8, bf16[4,256,4,256]{3,1,0,2:T(8,128)(2,1)} %bitcast.37), kind=kOutput, calls=%fused_computation.20 | convolution fusion | flops 537919488 | bytes 6291456 | tf_op jit(solution)/shard_map/gcir,igjr->cigj/dot_general | solution.py:58
  198.9 4.5 %copy.58 = bf16[256,16,256]{2,1,0:T(8,128)(2,1)} copy(bf16[256,16,256]{0,2,1:T(8,128)(2,1)} %bitcast.39) | data formatting | bytes 4194304 | tf_op jit(solution)/shard_map/convert_element_type | solution.py:62
  203.5 0.0 reduce-scatter.5.cloned.1.call-update
  203.5 0.2 reduce-scatter.3.cloned.1.call-start
  203.7 40.6 %all-to-all-done.2 = bf16[1024,4,256]{2,1,0:T(4,128)(2,1)} async-done(((bf16[1024,4,256]{2,1,0:T(4,128)(2,1)}), bf16[1024,4,256]{2,1,0:T(4,128)(2,1)}, u32[]{:S(2)}, u32[]{:S(2)}) %all-to-all-start.2) | async-done | bytes 2097184 | tf_op jit(solution)/shard_map/all_to_all | solution.py:70
  244.3 1.9 copy.54
  246.2 0.6 convert_bitcast_fusion
  246.8 4.7 %copy.55 = f32[16,64,4,256]{3,2,1,0:T(4,128)} copy(f32[16,64,4,256]{3,0,1,2:T(8,128)S(1)} %convert_bitcast_fusion) | data formatting | bytes 8388608 | tf_op jit(solution)/shard_map/convert_element_type | solution.py:71
  251.4 5.4 %reshape.33 = f32[16,256,256]{2,1,0:T(8,128)} reshape(f32[16,64,4,256]{3,2,1,0:T(4,128)} %copy.55) | data formatting | bytes 8388608 | tf_op jit(solution)/shard_map/convert_element_type | solution.py:71
  256.8 7.8 %convert_bitcast_fusion.1 = bf16[256,16,256]{0,2,1:T(8,128)(2,1)} fusion(bf16[16,256,256]{2,1,0:T(8,128)(2,1)S(1)} %bitcast.35, f32[16,256,256]{2,1,0:T(8,128)} %reshape.33, f32[16,256,256]{2,1,0:T(8,128)} %get-tuple-element.7), kind=kOutput, calls=%fused_computation.17 | convolution fusion | flops 557842432 | bytes 12582912 | tf_op jit(solution)/shard_map/bkr,bir->kbi/dot_general | solution.py:73
  264.6 4.6 %copy.56 = bf16[256,16,256]{2,1,0:T(8,128)(2,1)} copy(bf16[256,16,256]{0,2,1:T(8,128)(2,1)} %convert_bitcast_fusion.1) | data formatting | bytes 4194304 | tf_op jit(solution)/shard_map/convert_element_type | solution.py:73
  269.2 0.0 reduce-scatter.3.cloned.1.call-update
  269.2 4.8 %reduce-scatter.5.cloned.1.call-done = bf16[32,16,256]{2,1,0:T(8,128)(2,1)} async-done(((bf16[256,16,256]{2,1,0:T(8,128)(2,1)}), bf16[32,16,256]{2,1,0:T(8,128)(2,1)}) %reduce-scatter.5.cloned.1.call-update) | async-done | bytes 262160 | tf_op jit(solution)/shard_map/reduce_scatter | solution.py:61
  274.0 46.0 %reduce-scatter.3.cloned.1.call-done = bf16[32,16,256]{2,1,0:T(8,128)(2,1)} async-done(((bf16[256,16,256]{2,1,0:T(8,128)(2,1)}), bf16[32,16,256]{2,1,0:T(8,128)(2,1)}) %reduce-scatter.3.cloned.1.call-update) | async-done | bytes 262160 | tf_op jit(solution)/shard_map/reduce_scatter | solution.py:72
Async XLA Ops:
  7.2 75.7 %copy-start = (bf16[4096,256]{1,0:T(8,128)(2,1)S(1)}, bf16[4096,256]{1,0:T(8,128)(2,1)}, u32[]{:S(2)}) copy-start(bf16[4096,256]{1,0:T(8,128)(2,1)} %param.4) | copy-start | bytes 6291460
  7.2 75.7 %all-gather.3.cloned.1.call-start = ((), (), s32[]{:S(2)}) async-start(), calls=%async_computation.5 | async-start | bytes 2359296 | tf_op jit(solution)/shard_map/all_gather | solution.py:35
  10.2 1.6 copy-start.3
  11.8 78.8 %all-to-all-start.1 = ((bf16[8,32,16,256]{3,1,2,0:T(8,128)(2,1)}), bf16[8,32,16,256]{3,1,2,0:T(8,128)(2,1)}, u32[]{:S(2)}, u32[]{:S(2)}) async-start(bf16[8,32,16,256]{3,1,2,0:T(8,128)(2,1)} %stack.2), calls=%async_computation.1 | async-start | bytes 4194304 | tf_op jit(solution)/shard_map/all_to_all | solution.py:42
  90.6 67.4 %all-to-all-start = ((bf16[16,256,256]{2,0,1:T(8,128)(2,1)}), bf16[16,256,256]{2,0,1:T(8,128)(2,1)}, u32[]{:S(2)}, u32[]{:S(2)}) async-start(bf16[16,256,256]{2,0,1:T(8,128)(2,1)} %copy.43), calls=%async_computation | async-start | bytes 4194304 | tf_op jit(solution)/shard_map/all_to_all | solution.py:38
  107.0 67.1 %all-gather.5.cloned.1.call-start = ((), (), s32[]{:S(2)}) async-start(), calls=%async_computation.6 | async-start | bytes 2359296 | tf_op jit(solution)/shard_map/all_gather | solution.py:51
  158.0 3.3 copy-start.2
  159.9 1.3 copy-start.1
  180.2 64.1 %all-to-all-start.2 = ((bf16[1024,4,256]{2,1,0:T(4,128)(2,1)}), bf16[1024,4,256]{2,1,0:T(4,128)(2,1)}, u32[]{:S(2)}, u32[]{:S(2)}) async-start(bf16[1024,4,256]{2,1,0:T(4,128)(2,1)} %copy.53), calls=%async_computation.2 | async-start | bytes 4194304 | tf_op jit(solution)/shard_map/all_to_all | solution.py:70
  194.6 79.4 %reduce-scatter.5.cloned.1.call-start = ((), (), s32[]{:S(2)}) async-start(), calls=%async_computation.8 | async-start | bytes 2359296 | tf_op jit(solution)/shard_map/reduce_scatter | solution.py:61
  203.5 116.6 %reduce-scatter.3.cloned.1.call-start = ((), (), s32[]{:S(2)}) async-start(), calls=%async_computation.7 | async-start | bytes 2359296 | tf_op jit(solution)/shard_map/reduce_scatter | solution.py:72
Sparse Core Ops, SparseCore 0:
  10.7 72.1 all-gather.2
  110.5 63.5 all-gather.4
  203.6 70.3 reduce-scatter.4
  277.3 42.7 reduce-scatter.2
